TPU v7x, 256 devices: a whole 4x4x8 slice. The times are simulated.
256 devices in a mesh: expert: 16 (over z, core), tensor: 16 (over y, x).
Axes of the slice: x: 4, y: 4, z: 8, core: 2. Of those that a mesh axis runs over, the one named last changes fastest.
Arguments:
- residual_in: bfloat16 [22528, 1024], P(('expert', 'tensor')), may hold values from -6 to 6
- attn_heads: bfloat16 [1024, 22528], P('tensor', 'expert'), may hold values from -6 to 6
- out_proj: bfloat16 [1024, 1024], P('tensor'), may hold values from -0.1875 to 0.1875
- gain_first: float32 [1024], replicated, may hold values from 0.25 to 1.75
- router_weight: float32 [1024, 16], replicated, may hold values from -0.046875 to 0.046875
- routes: int32 [22528, 2], P(('expert', 'tensor')), may hold values from 0 to 15, all different within a row; in each aligned block of 88 rows (0 to 87, 88 to 175, ...) at most 22 rows name the same one
- w_gate: bfloat16 [16, 2816, 1024], P('expert', 'tensor'), may hold values from -0.1875 to 0.1875
- w_upward: bfloat16 [16, 2816, 1024], P('expert', 'tensor'), may hold values from -0.1875 to 0.1875
- w_downward: bfloat16 [16, 2816, 1024], P('expert', 'tensor'), may hold values from -0.21875 to 0.21875
- gain_second: float32 [1024], replicated, may hold values from 0.25 to 1.75
Outputs:
- residual_out: bfloat16 [22528, 1024], P(('expert', 'tensor'))
- next_normed: bfloat16 [22528, 1024], P(('expert', 'tensor'))
Inputs may be any that keep to these rules, and one draw needn't show every extreme that they name: `routes`: each row names two different experts; among the rows of one device no expert is named more than 22 times, and some expert reaches 22.
All inputs are finite; a program needn't handle non-finite values.
Results may differ from a plain program's by a relative error of at most 0.012.
Values may be sent and summed in bfloat16 or wider, within the bound.
No kernel may reach another device: no remote copies, remote signals or barrier semaphores. Data moves between devices by JAX's collectives and lax.ppermute only.
A program may use at most 128 MiB of HBM per device.

v0:
```python
import jax
import jax.numpy as jnp
from jax import lax
from jax.sharding import PartitionSpec as P


def rms_scale(values, gain):
    wide = values.astype(jnp.float32)
    scale = lax.rsqrt(jnp.mean(wide * wide, axis=-1, keepdims=True) + 1e-06)
    return (wide * scale * gain).astype(jnp.bfloat16)


def expert_block(inputs, gate_rows, up_rows, down_rows):
    gate_part = lax.dot_general(
        inputs, gate_rows, (((1,), (1,)), ((), ())), preferred_element_type=jnp.float32
    )
    up_part = lax.dot_general(
        inputs, up_rows, (((1,), (1,)), ((), ())), preferred_element_type=jnp.float32
    )
    hid = (jax.nn.gelu(gate_part, approximate=True) * up_part).astype(jnp.bfloat16)
    return jnp.dot(hid, down_rows, preferred_element_type=jnp.float32)


def per_device(
    residual_in,
    attn_heads,
    out_proj,
    gain_first,
    router_weight,
    routes,
    w_gate,
    w_upward,
    w_downward,
    gain_second,
):
    row_count = residual_in.shape[0]
    width = residual_in.shape[1]
    n_expert = lax.axis_size("expert")
    capacity = 4 * row_count // n_expert
    block = attn_heads
    projected = lax.psum_scatter(
        lax.dot_general(
            block, out_proj, (((0,), (0,)), ((), ())), preferred_element_type=jnp.float32
        ),
        "tensor",
        scatter_dimension=0,
        tiled=True,
    )
    hidden_one = (residual_in.astype(jnp.float32) + projected).astype(jnp.bfloat16)
    normed = rms_scale(hidden_one, gain_first)
    logits = jnp.dot(normed.astype(jnp.float32), router_weight, precision=lax.Precision.HIGHEST)
    router_probs = jax.nn.softmax(logits, axis=-1)
    picked = jnp.take_along_axis(router_probs, routes, axis=1)
    gate_weights = picked / jnp.sum(picked, axis=1, keepdims=True)
    flat_ids = routes.reshape(-1)
    expert_iota = jnp.arange(n_expert, dtype=jnp.int32)
    onehot = (flat_ids[:, None] == expert_iota[None, :]).astype(jnp.int32)
    earlier = jnp.cumsum(onehot, axis=0) - onehot
    slot_index = jnp.sum(earlier * onehot, axis=1)
    target = flat_ids * capacity + slot_index
    slot_iota = jnp.arange(n_expert * capacity, dtype=jnp.int32)
    placing = (slot_iota[:, None] == target[None, :]).astype(jnp.bfloat16)
    repeated = jnp.repeat(normed, 2, axis=0)
    send_slots = jnp.dot(placing, repeated, preferred_element_type=jnp.float32).astype(jnp.bfloat16)
    send_slots = send_slots.reshape(n_expert, capacity, width)
    received = lax.all_to_all(send_slots, "expert", split_axis=0, concat_axis=0, tiled=True)
    slot_total = n_expert * capacity
    rows_in = received.reshape(slot_total, width)
    gate_rows = w_gate[0]
    up_rows = w_upward[0]
    down_rows = w_downward[0]
    all_rows = lax.all_gather(rows_in, "tensor", axis=0, tiled=True)
    block = all_rows
    expert_sum = lax.psum_scatter(
        expert_block(block, gate_rows, up_rows, down_rows).astype(jnp.bfloat16),
        "tensor",
        scatter_dimension=0,
        tiled=True,
    )
    expert_out = expert_sum.reshape(n_expert, capacity, width)
    returned = lax.all_to_all(expert_out, "expert", split_axis=0, concat_axis=0, tiled=True)
    returned = returned.reshape(slot_total, width)
    per_route = lax.dot_general(
        placing, returned, (((0,), (0,)), ((), ())), preferred_element_type=jnp.float32
    )
    per_route = per_route.reshape(row_count, 2, width)
    mixed = jnp.sum(gate_weights[:, :, None] * per_route, axis=1)
    residual_out = (hidden_one.astype(jnp.float32) + mixed).astype(jnp.bfloat16)
    next_normed = rms_scale(residual_out, gain_second)
    return (residual_out, next_normed)


def solution(mesh):
    placed = (
        P(("expert", "tensor"), None),
        P("tensor", "expert"),
        P("tensor", None),
        P(),
        P(),
        P(("expert", "tensor"), None),
        P("expert", "tensor", None),
        P("expert", "tensor", None),
        P("expert", "tensor", None),
        P(),
    )
    return jax.shard_map(
        per_device,
        mesh=mesh,
        in_specs=placed,
        out_specs=(P(("expert", "tensor"), None), P(("expert", "tensor"), None)),
        check_vma=False,
    )
```

profile of v0, /device:TPU:1, one launch (start us, length us, event | category | flops | bytes accessed | tf_op | source)
XLA Modules:
  0.0 380.7 jit_solution(14872669456772548435)
XLA Ops:
  7.2 4.4 %fusion.38 = f32[1408,1024]{1,0:T(8,128)} fusion(bf16[64,1408]{1,0:T(8,128)(2,1)} %param.11, bf16[64,1024]{1,0:T(8,128)(2,1)} %param.12), kind=kOutput, calls=%fused_computation.66 | convolution fusion | flops 184549376 | bytes 6078464 | tf_op jit(solution)/shard_map/dot_general | solution.py:42
  11.7 0.6 copy-done.5
  12.3 0.1 copy.34
  12.4 0.1 reshape.109
  12.6 0.6 reduce-window.6
  13.2 0.2 slice_reduce_fusion
  13.5 86.2 %reduce-scatter.7.cloned.1.call-done = f32[88,1024]{1,0:T(8,128)} async-done(((f32[1408,1024]{1,0:T(8,128)}), f32[88,1024]{1,0:T(8,128)}) %reduce-scatter.7.cloned.1.call-update) | async-done | bytes 360464
  99.7 1.1 fusion.16
  100.9 0.1 fusion.18
  101.0 0.2 broadcast_in_dim.7
  101.2 0.1 reshape.112
  101.4 0.3 convolution_convert_fusion.1
  101.7 0.2 reshape.113
  101.9 32.1 %all_to_all.10 = bf16[16,22,1024]{2,1,0:T(8,128)(2,1)S(1)} all-to-all(bf16[16,22,1024]{2,1,0:T(8,128)(2,1)S(1)} %reshape.113), channel_id=1, replica_groups=mesh['expert'=16,'tensor'=16] {'expert'}, dimensions={0} | all-to-all | bytes 1441792 | tf_op jit(solution)/shard_map/all_to_all | solution.py:66
  134.1 1.1 reshape.114
  135.2 84.5 %all-gather.2.cloned.1.call-done = bf16[5632,1024]{1,0:T(8,128)(2,1)} async-done(((bf16[352,1024]{1,0:T(8,128)(2,1)}), bf16[5632,1024]{1,0:T(8,128)(2,1)}) %all-gather.2.cloned.1.call-update) | async-done | bytes 11534352 | tf_op jit(solution)/shard_map/all_gather | solution.py:72
  219.7 10.2 %fusion.23 = f32[5632,176]{0,1:T(8,128)} fusion(bf16[5632,1024]{1,0:T(8,128)(2,1)} %all-gather.2.cloned.1.call-done, bf16[1,176,1024]{2,1,0:T(8,128)(2,1)S(1)} %copy-done.2), kind=kOutput, calls=%fused_computation.33 | convolution fusion | flops 2030043136 | bytes 15859712 | tf_op jit(solution)/shard_map/dot_general | solution.py:14
  229.9 13.1 %convolution_convert_fusion = bf16[5632,1024]{1,0:T(8,128)(2,1)} fusion(bf16[5632,1024]{1,0:T(8,128)(2,1)} %all-gather.2.cloned.1.call-done, f32[5632,176]{0,1:T(8,128)} %fusion.23, bf16[1,176,1024]{2,1,0:T(8,128)(2,1)S(1)} %copy-done, bf16[1,176,1024]{2,1,0:T(8,128)(2,1)S(1)} %copy-done.8), kind=kOutput, calls=%fused_computation.1 | convolution fusion | flops 4075765760 | bytes 27754496 | tf_op jit(solution)/shard_map/dot_general | solution.py:21
  243.0 96.4 %reduce-scatter.5.cloned.1.call-done = bf16[352,1024]{1,0:T(8,128)(2,1)} async-done(((bf16[5632,1024]{1,0:T(8,128)(2,1)}), bf16[352,1024]{1,0:T(8,128)(2,1)}) %reduce-scatter.5.cloned.1.call-update) | async-done | bytes 720912 | tf_op jit(solution)/shard_map/reduce_scatter | solution.py:74
  339.5 2.1 reshape.115
  341.6 8.3 %all-to-all-start.1 = ((bf16[16,22,1024]{2,1,0:T(8,128)(2,1)}), bf16[16,22,1024]{2,1,0:T(8,128)(2,1)S(1)}, u32[]{:S(2)}, u32[]{:S(2)}) async-start(bf16[16,22,1024]{2,1,0:T(8,128)(2,1)} %reshape.115), calls=%async_computation.2 | async-start | bytes 1572864 | tf_op jit(solution)/shard_map/all_to_all | solution.py:81
  349.9 0.1 copy.32
  350.0 0.1 reshape.118
  350.1 0.1 iota_compare_fusion.2
  350.4 0.3 fusion.37
  350.7 2.3 gather_fusion
  353.0 0.1 reshape.121
  353.2 19.4 %all-to-all-done.1 = bf16[16,22,1024]{2,1,0:T(8,128)(2,1)S(1)} async-done(((bf16[16,22,1024]{2,1,0:T(8,128)(2,1)}), bf16[16,22,1024]{2,1,0:T(8,128)(2,1)S(1)}, u32[]{:S(2)}, u32[]{:S(2)}) %all-to-all-start.1) | async-done | bytes 720928 | tf_op jit(solution)/shard_map/all_to_all | solution.py:81
  372.6 0.2 reshape.129
  372.8 0.4 fusion.12
  373.2 0.2 fusion.13
  373.4 0.8 fusion.15
  (39 shorter events, 0.6 us)
Async XLA Ops:
  7.2 222.7 %copy-start = (bf16[1,176,1024]{2,1,0:T(8,128)(2,1)S(1)}, bf16[1,176,1024]{2,1,0:T(8,128)(2,1)}, u32[]{:S(2)}) copy-start(bf16[1,176,1024]{2,1,0:T(8,128)(2,1)} %param.18) | copy-start | bytes 1081348
  7.2 92.5 %reduce-scatter.7.cloned.1.call-start = ((), (), s32[]{:S(2)}) async-start(), calls=%async_computation.6 | async-start | bytes 6127616
  11.7 0.7 copy-start.5
  11.7 88.1 %copy-start.3 = (bf16[88,1024]{1,0:T(8,128)(2,1)S(1)}, bf16[88,1024]{1,0:T(8,128)(2,1)}, u32[]{:S(2)}) copy-start(bf16[88,1024]{1,0:T(8,128)(2,1)} %param.10) | copy-start | bytes 540676
  11.7 89.2 %copy-start.6 = (f32[1024]{0:T(1024)S(1)}, f32[1024]{0:T(1024)}, u32[]{:S(2)}) copy-start(f32[1024]{0:T(1024)} %param.13) | copy-start | bytes 12292
  11.7 208.0 %all-gather.2.cloned.1.call-start = ((), (), s32[]{:S(2)}) async-start(), calls=%async_computation.4 | async-start | bytes 12255232 | tf_op jit(solution)/shard_map/all_gather | solution.py:72
  100.9 118.8 %copy-start.2 = (bf16[1,176,1024]{2,1,0:T(8,128)(2,1)S(1)}, bf16[1,176,1024]{2,1,0:T(8,128)(2,1)}, u32[]{:S(2)}) copy-start(bf16[1,176,1024]{2,1,0:T(8,128)(2,1)} %param.16) | copy-start | bytes 1081348
  135.1 94.8 %copy-start.8 = (bf16[1,176,1024]{2,1,0:T(8,128)(2,1)S(1)}, bf16[1,176,1024]{2,1,0:T(8,128)(2,1)}, u32[]{:S(2)}) copy-start(bf16[1,176,1024]{2,1,0:T(8,128)(2,1)} %param.17) | copy-start | bytes 1081348
  135.2 204.3 %reduce-scatter.5.cloned.1.call-start = ((), (), s32[]{:S(2)}) async-start(), calls=%async_computation.5 | async-start | bytes 12255232 | tf_op jit(solution)/shard_map/reduce_scatter | solution.py:74
  243.0 107.4 %copy-start.4 = (f32[1024,16]{0,1:T(8,128)S(1)}, f32[1024,16]{0,1:T(8,128)}, u32[]{:S(2)}) copy-start(f32[1024,16]{0,1:T(8,128)} %param.14) | copy-start | bytes 196612
  341.6 31.1 %all-to-all-start.1 = ((bf16[16,22,1024]{2,1,0:T(8,128)(2,1)}), bf16[16,22,1024]{2,1,0:T(8,128)(2,1)S(1)}, u32[]{:S(2)}, u32[]{:S(2)}) async-start(bf16[16,22,1024]{2,1,0:T(8,128)(2,1)} %reshape.115), calls=%async_computation.2 | async-start | bytes 1572864 | tf_op jit(solution)/shard_map/all_to_all | solution.py:81
  350.7 22.7 %copy-start.7 = (f32[1024]{0:T(1024)S(1)}, f32[1024]{0:T(1024)}, u32[]{:S(2)}) copy-start(f32[1024]{0:T(1024)} %param.19) | copy-start | bytes 12292
  373.3 0.8 copy-start.1
Sparse Core Ops, SparseCore 0:
  11.8 87.8 reduce-scatter.6
  135.3 84.3 all-gather.1
  243.2 96.2 reduce-scatter.4
where the time goes:
time: 381 us
  waiting for transfers between devices  287 us (75%)
  blocking collectives  32.1 us (8%)
  matrix products  28.7 us (8%)
  between operations  14 us (4%)
  starting transfers between devices  8.46 us (2%)
  local copies, waits for them, and re-layouts  7.73 us (2%)
    reduce_scatter x1, waiting for transfers between devices, per_device(): lax.psum_scatter(expert_block(block, gate_rows, up_rows, down_rows).astyp...  96.4 us
    unnamed x4, waiting for transfers between devices  86.2 us
    all_gather x1, waiting for transfers between devices, per_device(): all_rows = lax.all_gather(rows_in, 'tensor', axis=0, tiled=True)  84.5 us
    all_to_all x1, blocking collectives, per_device(): lax.all_to_all(send_slots, 'expert', split_axis=0, concat_axis=0, tiled=T...  32.1 us
    all_to_all x1, waiting for transfers between devices, per_device(): lax.all_to_all(expert_out, 'expert', split_axis=0, concat_axis=0, tiled=T...  19.4 us
    dot_general x1, matrix products, expert_block(): return jnp.dot(hid, down_rows, preferred_element_type=jnp.float32)  13.1 us
    dot_general x1, matrix products, expert_block(): lax.dot_general(inputs, gate_rows, (((1,), (1,)), ((), ())), preferred_el...  10.2 us
    all_to_all x1, starting transfers between devices, per_device(): lax.all_to_all(expert_out, 'expert', split_axis=0, concat_axis=0, tiled=T...  8.33 us
  transfers between devices with their start and end apart: 4, of which 4 were waited for; matrix products, arithmetic and copies ran while one was open for 1% of the time, Pallas kernels for 0%

commit v1 on v0

--- a/solution.py
+++ b/solution.py
@@ -2,6 +2,12 @@
 import jax.numpy as jnp
 from jax import lax
 from jax.sharding import PartitionSpec as P
+
+
+def in_order(blocks, dim):
+    blocks = jnp.moveaxis(blocks, 0, dim)
+    shape = blocks.shape
+    return blocks.reshape(*shape[:dim], shape[dim] * shape[dim + 1], *shape[dim + 2 :])
 
 
 def rms_scale(values, gain):
@@ -69,7 +75,19 @@
     gate_rows = w_gate[0]
     up_rows = w_upward[0]
     down_rows = w_downward[0]
-    all_rows = lax.all_gather(rows_in, "tensor", axis=0, tiled=True)
+    size = lax.axis_size("tensor")
+    pairs = [(i, (i + 1) % size) for i in range(size)]
+    back = [(b, a) for a, b in pairs]
+    lower, upper = ([], [])
+    for lap in range(size - 1):
+        if lap % 2 == 0:
+            lower.append(lax.ppermute(lower[-1] if lower else rows_in, "tensor", pairs))
+        else:
+            upper.append(lax.ppermute(upper[-1] if upper else rows_in, "tensor", back))
+    blocks = jnp.stack([*lower[::-1], rows_in, *upper])
+    shift = lax.axis_index("tensor") - len(lower)
+    blocks = blocks[(jnp.arange(size) - shift) % size]
+    all_rows = in_order(blocks, 0)
     block = all_rows
     expert_sum = lax.psum_scatter(
         expert_block(block, gate_rows, up_rows, down_rows).astype(jnp.bfloat16),

time: 381 us -> 476 us (1.25)
  starting transfers between devices: 8.46 us -> 44 us
  local copies, waits for them, and re-layouts: 7.73 us -> 42.8 us
  waiting for transfers between devices: 287 us -> 310 us
    ppermute x0 -> x15, waiting for transfers between devices: none -> 111 us  [the longest x8 111 us: per_device(): lower.append(lax.ppermute(lower[-1] if lower else rows_in, 'tensor', pairs))]
    all_gather x1 -> x0, waiting for transfers between devices: 84.5 us -> none  [per_device(): all_rows = lax.all_gather(rows_in, 'tensor', axis=0, tiled=True)]
    ppermute x0 -> x15, starting transfers between devices: none -> 35.6 us  [the longest x7 34.6 us: per_device(): upper.append(lax.ppermute(upper[-1] if upper else rows_in, 'tensor', back))]
    unnamed x19 -> x62, local copies, waits for them, and re-layouts: 0.74 us -> 25.1 us
    gather x0 -> x1, local copies, waits for them, and re-layouts: none -> 10.4 us  [per_device(): blocks = blocks[(jnp.arange(size) - shift) % size]]
    unnamed x4 -> x3, waiting for transfers between devices: 86.2 us -> 86.6 us
  transfers between devices with their start and end apart: 4 -> 18, of which waited for: 4 -> 11; matrix products, arithmetic and copies ran while one was open for 1% -> 6% of each run, Pallas kernels for 0% -> 0%
where the time goes in v1:
time: 476 us
  waiting for transfers between devices  310 us (65%)
  starting transfers between devices  44 us (9%)
  local copies, waits for them, and re-layouts  42.8 us (9%)
  blocking collectives  32.1 us (7%)
  matrix products  28.9 us (6%)
  between operations  14.4 us (3%)
    ppermute x8, waiting for transfers between devices, per_device(): lower.append(lax.ppermute(lower[-1] if lower else rows_in, 'tensor', pairs))  111 us
    reduce_scatter x1, waiting for transfers between devices, per_device(): lax.psum_scatter(expert_block(block, gate_rows, up_rows, down_rows).astyp...  93.4 us
    unnamed x3, waiting for transfers between devices  86.6 us
    ppermute x7, starting transfers between devices, per_device(): upper.append(lax.ppermute(upper[-1] if upper else rows_in, 'tensor', back))  34.6 us
    all_to_all x1, blocking collectives, per_device(): lax.all_to_all(send_slots, 'expert', split_axis=0, concat_axis=0, tiled=T...  32.1 us
    unnamed x62, local copies, waits for them, and re-layouts  25.1 us
    all_to_all x1, waiting for transfers between devices, per_device(): lax.all_to_all(expert_out, 'expert', split_axis=0, concat_axis=0, tiled=T...  19.4 us
    dot_general x1, matrix products, expert_block(): return jnp.dot(hid, down_rows, preferred_element_type=jnp.float32)  13.1 us
  transfers between devices with their start and end apart: 18, of which 11 were waited for; matrix products, arithmetic and copies ran while one was open for 6% of the time, Pallas kernels for 0%

profile of v1, /device:TPU:1, one launch (start us, length us, event | category | flops | bytes accessed | tf_op | source)
XLA Modules:
  0.0 475.5 jit_solution(2142085877555331518)
XLA Ops:
  7.3 4.5 fusion.40
  13.1 86.5 %reduce-scatter.7.cloned.1.call-done = f32[88,1024]{1,0:T(8,128)} async-done(((f32[1408,1024]{1,0:T(8,128)}), f32[88,1024]{1,0:T(8,128)}) %reduce-scatter.7.cloned.1.call-update) | async-done | bytes 360464
  101.8 32.1 %all_to_all.10 = bf16[16,22,1024]{2,1,0:T(8,128)(2,1)S(1)} all-to-all(bf16[16,22,1024]{2,1,0:T(8,128)(2,1)S(1)} %reshape.165), channel_id=1, replica_groups=mesh['expert'=16,'tensor'=16] {'expert'}, dimensions={0} | all-to-all | bytes 1441792 | tf_op jit(solution)/shard_map/all_to_all | solution.py:72
  135.1 20.5 %collective-permute-done = bf16[352,1024]{1,0:T(8,128)(2,1)S(1)} collective-permute-done((bf16[352,1024]{1,0:T(8,128)(2,1)S(1)}, bf16[352,1024]{1,0:T(8,128)(2,1)S(1)}, u32[]{:S(2)}, u32[]{:S(2)}) %collective-permute-start) | collective-permute-done | bytes 720928 | tf_op jit(solution)/shard_map/ppermute | solution.py:84
  155.6 4.8 %collective-permute-start.8 = (bf16[352,1024]{1,0:T(8,128)(2,1)}, bf16[352,1024]{1,0:T(8,128)(2,1)S(1)}, u32[]{:S(2)}, u32[]{:S(2)}) collective-permute-start(bf16[352,1024]{1,0:T(8,128)(2,1)} %copy-done.14), channel_id=1, source_target_pairs={{1,0},{2,1},{3,2},{4,3},{5,4},{6,5},{7,6},{8,7},{9,8},{10,9},{11,1... | collective-permute-start | bytes 2162696 | tf_op jit(solution)/shard_map/ppermute | solution.py:86
  160.4 15.7 %collective-permute-done.1 = bf16[352,1024]{1,0:T(8,128)(2,1)S(1)} collective-permute-done((bf16[352,1024]{1,0:T(8,128)(2,1)S(1)}, bf16[352,1024]{1,0:T(8,128)(2,1)S(1)}, u32[]{:S(2)}, u32[]{:S(2)}) %collective-permute-start.1) | collective-permute-done | bytes 720928 | tf_op jit(solution)/shard_map/ppermute | solution.py:84
  176.2 4.8 %collective-permute-start.9 = (bf16[352,1024]{1,0:T(8,128)(2,1)S(1)}, bf16[352,1024]{1,0:T(8,128)(2,1)S(1)}, u32[]{:S(2)}, u32[]{:S(2)}) collective-permute-start(bf16[352,1024]{1,0:T(8,128)(2,1)S(1)} %collective-permute-done.8), channel_id=1, source_target_pairs={{1,0},{2,1},{3,2},{4,3},{5,4},{6,5},{7,6},{8,7},{9,8},{10,9},{11,1... | collective-permute-start | bytes 2162696 | tf_op jit(solution)/shard_map/ppermute | solution.py:86
  180.9 14.9 %collective-permute-done.2 = bf16[352,1024]{1,0:T(8,128)(2,1)S(1)} collective-permute-done((bf16[352,1024]{1,0:T(8,128)(2,1)S(1)}, bf16[352,1024]{1,0:T(8,128)(2,1)S(1)}, u32[]{:S(2)}, u32[]{:S(2)}) %collective-permute-start.2) | collective-permute-done | bytes 720928 | tf_op jit(solution)/shard_map/ppermute | solution.py:84
  195.8 4.8 %collective-permute-start.10 = (bf16[352,1024]{1,0:T(8,128)(2,1)S(1)}, bf16[352,1024]{1,0:T(8,128)(2,1)S(1)}, u32[]{:S(2)}, u32[]{:S(2)}) collective-permute-start(bf16[352,1024]{1,0:T(8,128)(2,1)S(1)} %collective-permute-done.9), channel_id=1, source_target_pairs={{1,0},{2,1},{3,2},{4,3},{5,4},{6,5},{7,6},{8,7},{9,8},{10,9},{11,1... | collective-permute-start | bytes 2162696 | tf_op jit(solution)/shard_map/ppermute | solution.py:86
  200.7 14.0 %collective-permute-done.3 = bf16[352,1024]{1,0:T(8,128)(2,1)S(1)} collective-permute-done((bf16[352,1024]{1,0:T(8,128)(2,1)S(1)}, bf16[352,1024]{1,0:T(8,128)(2,1)S(1)}, u32[]{:S(2)}, u32[]{:S(2)}) %collective-permute-start.3) | collective-permute-done | bytes 720928 | tf_op jit(solution)/shard_map/ppermute | solution.py:84
  214.7 4.8 %collective-permute-start.11 = (bf16[352,1024]{1,0:T(8,128)(2,1)S(1)}, bf16[352,1024]{1,0:T(8,128)(2,1)S(1)}, u32[]{:S(2)}, u32[]{:S(2)}) collective-permute-start(bf16[352,1024]{1,0:T(8,128)(2,1)S(1)} %collective-permute-done.10), channel_id=1, source_target_pairs={{1,0},{2,1},{3,2},{4,3},{5,4},{6,5},{7,6},{8,7},{9,8},{10,9},{11,1... | collective-permute-start | bytes 2162696 | tf_op jit(solution)/shard_map/ppermute | solution.py:86
  219.5 13.1 %collective-permute-done.4 = bf16[352,1024]{1,0:T(8,128)(2,1)S(1)} collective-permute-done((bf16[352,1024]{1,0:T(8,128)(2,1)S(1)}, bf16[352,1024]{1,0:T(8,128)(2,1)S(1)}, u32[]{:S(2)}, u32[]{:S(2)}) %collective-permute-start.4) | collective-permute-done | bytes 720928 | tf_op jit(solution)/shard_map/ppermute | solution.py:84
  233.6 4.7 collective-permute-start.12
  238.3 11.4 %collective-permute-done.5 = bf16[352,1024]{1,0:T(8,128)(2,1)S(1)} collective-permute-done((bf16[352,1024]{1,0:T(8,128)(2,1)S(1)}, bf16[352,1024]{1,0:T(8,128)(2,1)S(1)}, u32[]{:S(2)}, u32[]{:S(2)}) %collective-permute-start.5) | collective-permute-done | bytes 720928 | tf_op jit(solution)/shard_map/ppermute | solution.py:84
  249.7 5.5 %collective-permute-start.13 = (bf16[352,1024]{1,0:T(8,128)(2,1)}, bf16[352,1024]{1,0:T(8,128)(2,1)}, u32[]{:S(2)}, u32[]{:S(2)}) collective-permute-start(bf16[352,1024]{1,0:T(8,128)(2,1)} %collective-permute-done.12), channel_id=1, source_target_pairs={{1,0},{2,1},{3,2},{4,3},{5,4},{6,5},{7,6},{8,7},{9,8},{10,9},{11,1... | collective-permute-start | bytes 2162696 | tf_op jit(solution)/shard_map/ppermute | solution.py:86
  255.2 10.8 %collective-permute-done.6 = bf16[352,1024]{1,0:T(8,128)(2,1)} collective-permute-done((bf16[352,1024]{1,0:T(8,128)(2,1)S(1)}, bf16[352,1024]{1,0:T(8,128)(2,1)}, u32[]{:S(2)}, u32[]{:S(2)}) %collective-permute-start.6) | collective-permute-done | bytes 720928 | tf_op jit(solution)/shard_map/ppermute | solution.py:84
  266.4 5.1 %collective-permute-start.14 = (bf16[352,1024]{1,0:T(8,128)(2,1)}, bf16[352,1024]{1,0:T(8,128)(2,1)S(1)}, u32[]{:S(2)}, u32[]{:S(2)}) collective-permute-start(bf16[352,1024]{1,0:T(8,128)(2,1)} %collective-permute-done.13), channel_id=1, source_target_pairs={{1,0},{2,1},{3,2},{4,3},{5,4},{6,5},{7,6},{8,7},{9,8},{10,9},{11,1... | collective-permute-start | bytes 2162696 | tf_op jit(solution)/shard_map/ppermute | solution.py:86
  271.5 10.3 %collective-permute-done.7 = bf16[352,1024]{1,0:T(8,128)(2,1)} collective-permute-done((bf16[352,1024]{1,0:T(8,128)(2,1)}, bf16[352,1024]{1,0:T(8,128)(2,1)}, u32[]{:S(2)}, u32[]{:S(2)}) %collective-permute-start.7) | collective-permute-done | bytes 720928 | tf_op jit(solution)/shard_map/ppermute | solution.py:84
  283.8 2.0 bitcast_dynamic-update-slice_fusion.13
  285.8 2.0 bitcast_dynamic-update-slice_fusion.12
  287.9 2.0 bitcast_dynamic-update-slice_fusion.11
  291.9 2.0 bitcast_dynamic-update-slice_fusion.9
  294.0 2.0 bitcast_dynamic-update-slice_fusion.8
  303.7 2.0 bitcast_dynamic-update-slice_fusion.1
  306.7 10.4 %gather_fusion = bf16[16,352,1024]{2,1,0:T(8,128)(2,1)} fusion(bf16[16,352,1024]{2,1,0:T(8,128)(2,1)} %bitcast_dynamic-update-slice_fusion, s32[1024]{0:T(1024)S(1)} %pad_clamp_fusion), kind=kCustom, calls=%fused_computation | custom fusion | bytes 23068736 | tf_op jit(solution)/shard_map/gather | solution.py:89
  317.1 10.2 %fusion.23 = f32[5632,176]{0,1:T(8,128)} fusion(bf16[5632,1024]{1,0:T(8,128)(2,1)} %bitcast.68, bf16[1,176,1024]{2,1,0:T(8,128)(2,1)S(1)} %copy-done.16), kind=kOutput, calls=%fused_computation.49 | convolution fusion | flops 2030043136 | bytes 15859712 | tf_op jit(solution)/shard_map/dot_general | solution.py:20
  327.3 13.1 %convolution_convert_fusion = bf16[5632,1024]{1,0:T(8,128)(2,1)} fusion(bf16[5632,1024]{1,0:T(8,128)(2,1)} %bitcast.69, f32[5632,176]{0,1:T(8,128)} %fusion.23, bf16[1,176,1024]{2,1,0:T(8,128)(2,1)S(1)} %copy-done, bf16[1,176,1024]{2,1,0:T(8,128)(2,1)S(1)} %copy-done.22), kind=kOutput, calls=%fused_computation.2 | convolution fusion | flops 4075765760 | bytes 27754496 | tf_op jit(solution)/shard_map/dot_general | solution.py:27
  340.5 93.4 %reduce-scatter.5.cloned.1.call-done = bf16[352,1024]{1,0:T(8,128)(2,1)} async-done(((bf16[5632,1024]{1,0:T(8,128)(2,1)}), bf16[352,1024]{1,0:T(8,128)(2,1)}) %reduce-scatter.5.cloned.1.call-update) | async-done | bytes 720912 | tf_op jit(solution)/shard_map/reduce_scatter | solution.py:92
  434.0 2.1 reshape.168
  436.1 8.4 %all-to-all-start.1 = ((bf16[16,22,1024]{2,1,0:T(8,128)(2,1)}), bf16[16,22,1024]{2,1,0:T(8,128)(2,1)S(1)}, u32[]{:S(2)}, u32[]{:S(2)}) async-start(bf16[16,22,1024]{2,1,0:T(8,128)(2,1)} %reshape.168), calls=%async_computation.2 | async-start | bytes 1572864 | tf_op jit(solution)/shard_map/all_to_all | solution.py:99
  445.2 2.3 gather_fusion.1
  447.8 19.4 %all-to-all-done.1 = bf16[16,22,1024]{2,1,0:T(8,128)(2,1)S(1)} async-done(((bf16[16,22,1024]{2,1,0:T(8,128)(2,1)}), bf16[16,22,1024]{2,1,0:T(8,128)(2,1)S(1)}, u32[]{:S(2)}, u32[]{:S(2)}) %all-to-all-start.1) | async-done | bytes 720928 | tf_op jit(solution)/shard_map/all_to_all | solution.py:99
  (114 shorter events, 21.1 us)
Async XLA Ops:
  7.2 320.2 %copy-start = (bf16[1,176,1024]{2,1,0:T(8,128)(2,1)S(1)}, bf16[1,176,1024]{2,1,0:T(8,128)(2,1)}, u32[]{:S(2)}) copy-start(bf16[1,176,1024]{2,1,0:T(8,128)(2,1)} %param.18) | copy-start | bytes 1081348
  7.2 92.4 %copy-start.17 = (bf16[88,1024]{1,0:T(8,128)(2,1)S(1)}, bf16[88,1024]{1,0:T(8,128)(2,1)}, u32[]{:S(2)}) copy-start(bf16[88,1024]{1,0:T(8,128)(2,1)} %param.10) | copy-start | bytes 540676
  7.2 93.6 %copy-start.20 = (f32[1024]{0:T(1024)S(1)}, f32[1024]{0:T(1024)}, u32[]{:S(2)}) copy-start(f32[1024]{0:T(1024)} %param.13) | copy-start | bytes 12292
  7.2 92.4 %reduce-scatter.7.cloned.1.call-start = ((), (), s32[]{:S(2)}) async-start(), calls=%async_computation.5 | async-start | bytes 6127616
  11.8 422.2 %reduce-scatter.5.cloned.1.call-start = ((), (), s32[]{:S(2)}) async-start(), calls=%async_computation.4 | async-start | bytes 12255232 | tf_op jit(solution)/shard_map/reduce_scatter | solution.py:92
  134.1 21.5 %copy-start.14 = (bf16[352,1024]{1,0:T(8,128)(2,1)}, bf16[352,1024]{1,0:T(8,128)(2,1)S(1)}, u32[]{:S(2)}) copy-start(bf16[352,1024]{1,0:T(8,128)(2,1)S(1)} %reshape.166) | copy-start | bytes 2162692
  134.1 21.5 %collective-permute-start = (bf16[352,1024]{1,0:T(8,128)(2,1)S(1)}, bf16[352,1024]{1,0:T(8,128)(2,1)S(1)}, u32[]{:S(2)}, u32[]{:S(2)}) collective-permute-start(bf16[352,1024]{1,0:T(8,128)(2,1)S(1)} %reshape.166), channel_id=1, source_target_pairs={{0,1},{1,2},{2,3},{3,4},{4,5},{5,6},{6,7},{7,8},{8,9},{9,10},{10,1... | collective-permute-start | bytes 2162696 | tf_op jit(solution)/shard_map/ppermute | solution.py:84
  155.6 20.5 %collective-permute-start.1 = (bf16[352,1024]{1,0:T(8,128)(2,1)S(1)}, bf16[352,1024]{1,0:T(8,128)(2,1)S(1)}, u32[]{:S(2)}, u32[]{:S(2)}) collective-permute-start(bf16[352,1024]{1,0:T(8,128)(2,1)S(1)} %collective-permute-done), channel_id=1, source_target_pairs={{0,1},{1,2},{2,3},{3,4},{4,5},{5,6},{6,7},{7,8},{8,9},{9,10},{10,1... | collective-permute-start | bytes 2162696 | tf_op jit(solution)/shard_map/ppermute | solution.py:84
  155.6 20.5 %collective-permute-start.8 = (bf16[352,1024]{1,0:T(8,128)(2,1)}, bf16[352,1024]{1,0:T(8,128)(2,1)S(1)}, u32[]{:S(2)}, u32[]{:S(2)}) collective-permute-start(bf16[352,1024]{1,0:T(8,128)(2,1)} %copy-done.14), channel_id=1, source_target_pairs={{1,0},{2,1},{3,2},{4,3},{5,4},{6,5},{7,6},{8,7},{9,8},{10,9},{11,1... | collective-permute-start | bytes 2162696 | tf_op jit(solution)/shard_map/ppermute | solution.py:86
  176.1 19.7 %copy-start.3 = (bf16[352,1024]{1,0:T(8,128)(2,1)}, bf16[352,1024]{1,0:T(8,128)(2,1)S(1)}, u32[]{:S(2)}) copy-start(bf16[352,1024]{1,0:T(8,128)(2,1)S(1)} %collective-permute-done.1) | copy-start | bytes 2162692
  176.1 19.7 %collective-permute-start.2 = (bf16[352,1024]{1,0:T(8,128)(2,1)S(1)}, bf16[352,1024]{1,0:T(8,128)(2,1)S(1)}, u32[]{:S(2)}, u32[]{:S(2)}) collective-permute-start(bf16[352,1024]{1,0:T(8,128)(2,1)S(1)} %collective-permute-done.1), channel_id=1, source_target_pairs={{0,1},{1,2},{2,3},{3,4},{4,5},{5,6},{6,7},{7,8},{8,9},{9,10},{10,1... | collective-permute-start | bytes 2162696 | tf_op jit(solution)/shard_map/ppermute | solution.py:84
  176.1 90.0 %copy-start.1 = (bf16[352,1024]{1,0:T(8,128)(2,1)}, bf16[352,1024]{1,0:T(8,128)(2,1)S(1)}, u32[]{:S(2)}) copy-start(bf16[352,1024]{1,0:T(8,128)(2,1)S(1)} %collective-permute-done.8) | copy-start | bytes 2162692
  176.2 19.7 %collective-permute-start.9 = (bf16[352,1024]{1,0:T(8,128)(2,1)S(1)}, bf16[352,1024]{1,0:T(8,128)(2,1)S(1)}, u32[]{:S(2)}, u32[]{:S(2)}) collective-permute-start(bf16[352,1024]{1,0:T(8,128)(2,1)S(1)} %collective-permute-done.8), channel_id=1, source_target_pairs={{1,0},{2,1},{3,2},{4,3},{5,4},{6,5},{7,6},{8,7},{9,8},{10,9},{11,1... | collective-permute-start | bytes 2162696 | tf_op jit(solution)/shard_map/ppermute | solution.py:86
  195.8 18.8 %collective-permute-start.3 = (bf16[352,1024]{1,0:T(8,128)(2,1)S(1)}, bf16[352,1024]{1,0:T(8,128)(2,1)S(1)}, u32[]{:S(2)}, u32[]{:S(2)}) collective-permute-start(bf16[352,1024]{1,0:T(8,128)(2,1)S(1)} %collective-permute-done.2), channel_id=1, source_target_pairs={{0,1},{1,2},{2,3},{3,4},{4,5},{5,6},{6,7},{7,8},{8,9},{9,10},{10,1... | collective-permute-start | bytes 2162696 | tf_op jit(solution)/shard_map/ppermute | solution.py:84
  195.8 18.8 %collective-permute-start.10 = (bf16[352,1024]{1,0:T(8,128)(2,1)S(1)}, bf16[352,1024]{1,0:T(8,128)(2,1)S(1)}, u32[]{:S(2)}, u32[]{:S(2)}) collective-permute-start(bf16[352,1024]{1,0:T(8,128)(2,1)S(1)} %collective-permute-done.9), channel_id=1, source_target_pairs={{1,0},{2,1},{3,2},{4,3},{5,4},{6,5},{7,6},{8,7},{9,8},{10,9},{11,1... | collective-permute-start | bytes 2162696 | tf_op jit(solution)/shard_map/ppermute | solution.py:86
  214.6 35.1 %copy-start.11 = (bf16[352,1024]{1,0:T(8,128)(2,1)}, bf16[352,1024]{1,0:T(8,128)(2,1)S(1)}, u32[]{:S(2)}) copy-start(bf16[352,1024]{1,0:T(8,128)(2,1)S(1)} %collective-permute-done.3) | copy-start | bytes 2162692
  214.6 18.0 %collective-permute-start.4 = (bf16[352,1024]{1,0:T(8,128)(2,1)S(1)}, bf16[352,1024]{1,0:T(8,128)(2,1)S(1)}, u32[]{:S(2)}, u32[]{:S(2)}) collective-permute-start(bf16[352,1024]{1,0:T(8,128)(2,1)S(1)} %collective-permute-done.3), channel_id=1, source_target_pairs={{0,1},{1,2},{2,3},{3,4},{4,5},{5,6},{6,7},{7,8},{8,9},{9,10},{10,1... | collective-permute-start | bytes 2162696 | tf_op jit(solution)/shard_map/ppermute | solution.py:84
  214.7 17.9 %collective-permute-start.11 = (bf16[352,1024]{1,0:T(8,128)(2,1)S(1)}, bf16[352,1024]{1,0:T(8,128)(2,1)S(1)}, u32[]{:S(2)}, u32[]{:S(2)}) collective-permute-start(bf16[352,1024]{1,0:T(8,128)(2,1)S(1)} %collective-permute-done.10), channel_id=1, source_target_pairs={{1,0},{2,1},{3,2},{4,3},{5,4},{6,5},{7,6},{8,7},{9,8},{10,9},{11,1... | collective-permute-start | bytes 2162696 | tf_op jit(solution)/shard_map/ppermute | solution.py:86
  232.6 22.6 %copy-start.12 = (bf16[352,1024]{1,0:T(8,128)(2,1)}, bf16[352,1024]{1,0:T(8,128)(2,1)S(1)}, u32[]{:S(2)}) copy-start(bf16[352,1024]{1,0:T(8,128)(2,1)S(1)} %collective-permute-done.4) | copy-start | bytes 2162692
  232.6 17.1 %collective-permute-start.5 = (bf16[352,1024]{1,0:T(8,128)(2,1)S(1)}, bf16[352,1024]{1,0:T(8,128)(2,1)S(1)}, u32[]{:S(2)}, u32[]{:S(2)}) collective-permute-start(bf16[352,1024]{1,0:T(8,128)(2,1)S(1)} %collective-permute-done.4), channel_id=1, source_target_pairs={{0,1},{1,2},{2,3},{3,4},{4,5},{5,6},{6,7},{7,8},{8,9},{9,10},{10,1... | collective-permute-start | bytes 2162696 | tf_op jit(solution)/shard_map/ppermute | solution.py:84
  233.6 16.2 %collective-permute-start.12 = (bf16[352,1024]{1,0:T(8,128)(2,1)S(1)}, bf16[352,1024]{1,0:T(8,128)(2,1)}, u32[]{:S(2)}, u32[]{:S(2)}) collective-permute-start(bf16[352,1024]{1,0:T(8,128)(2,1)S(1)} %collective-permute-done.11), channel_id=1, source_target_pairs={{1,0},{2,1},{3,2},{4,3},{5,4},{6,5},{7,6},{8,7},{9,8},{10,9},{11,1... | collective-permute-start | bytes 2162696 | tf_op jit(solution)/shard_map/ppermute | solution.py:86
  249.7 16.4 %collective-permute-start.6 = (bf16[352,1024]{1,0:T(8,128)(2,1)S(1)}, bf16[352,1024]{1,0:T(8,128)(2,1)}, u32[]{:S(2)}, u32[]{:S(2)}) collective-permute-start(bf16[352,1024]{1,0:T(8,128)(2,1)S(1)} %collective-permute-done.5), channel_id=1, source_target_pairs={{0,1},{1,2},{2,3},{3,4},{4,5},{5,6},{6,7},{7,8},{8,9},{9,10},{10,1... | collective-permute-start | bytes 2162696 | tf_op jit(solution)/shard_map/ppermute | solution.py:84
  249.7 16.6 %collective-permute-start.13 = (bf16[352,1024]{1,0:T(8,128)(2,1)}, bf16[352,1024]{1,0:T(8,128)(2,1)}, u32[]{:S(2)}, u32[]{:S(2)}) collective-permute-start(bf16[352,1024]{1,0:T(8,128)(2,1)} %collective-permute-done.12), channel_id=1, source_target_pairs={{1,0},{2,1},{3,2},{4,3},{5,4},{6,5},{7,6},{8,7},{9,8},{10,9},{11,1... | collective-permute-start | bytes 2162696 | tf_op jit(solution)/shard_map/ppermute | solution.py:86
  266.1 15.7 %collective-permute-start.7 = (bf16[352,1024]{1,0:T(8,128)(2,1)}, bf16[352,1024]{1,0:T(8,128)(2,1)}, u32[]{:S(2)}, u32[]{:S(2)}) collective-permute-start(bf16[352,1024]{1,0:T(8,128)(2,1)} %collective-permute-done.6), channel_id=1, source_target_pairs={{0,1},{1,2},{2,3},{3,4},{4,5},{5,6},{6,7},{7,8},{8,9},{9,10},{10,1... | collective-permute-start | bytes 2162696 | tf_op jit(solution)/shard_map/ppermute | solution.py:84
  266.3 31.5 %copy-start.2 = (bf16[352,1024]{1,0:T(8,128)(2,1)S(1)}, bf16[352,1024]{1,0:T(8,128)(2,1)}, u32[]{:S(2)}) copy-start(bf16[352,1024]{1,0:T(8,128)(2,1)} %copy-done.1) | copy-start | bytes 2162692
  266.3 32.4 %copy-start.5 = (bf16[352,1024]{1,0:T(8,128)(2,1)S(1)}, bf16[352,1024]{1,0:T(8,128)(2,1)}, u32[]{:S(2)}) copy-start(bf16[352,1024]{1,0:T(8,128)(2,1)} %copy-done.4) | copy-start | bytes 2162692
  266.4 33.4 %copy-start.8 = (bf16[352,1024]{1,0:T(8,128)(2,1)S(1)}, bf16[352,1024]{1,0:T(8,128)(2,1)}, u32[]{:S(2)}) copy-start(bf16[352,1024]{1,0:T(8,128)(2,1)} %copy-done.7) | copy-start | bytes 2162692
  266.4 34.3 %copy-start.10 = (bf16[352,1024]{1,0:T(8,128)(2,1)S(1)}, bf16[352,1024]{1,0:T(8,128)(2,1)}, u32[]{:S(2)}) copy-start(bf16[352,1024]{1,0:T(8,128)(2,1)} %copy-done.9) | copy-start | bytes 2162692
  266.4 39.4 %collective-permute-start.14 = (bf16[352,1024]{1,0:T(8,128)(2,1)}, bf16[352,1024]{1,0:T(8,128)(2,1)S(1)}, u32[]{:S(2)}, u32[]{:S(2)}) collective-permute-start(bf16[352,1024]{1,0:T(8,128)(2,1)} %collective-permute-done.13), channel_id=1, source_target_pairs={{1,0},{2,1},{3,2},{4,3},{5,4},{6,5},{7,6},{8,7},{9,8},{10,9},{11,1... | collective-permute-start | bytes 2162696 | tf_op jit(solution)/shard_map/ppermute | solution.py:86
  340.5 104.4 %copy-start.18 = (f32[1024,16]{0,1:T(8,128)S(1)}, f32[1024,16]{0,1:T(8,128)}, u32[]{:S(2)}) copy-start(f32[1024,16]{0,1:T(8,128)} %param.14) | copy-start | bytes 196612
  436.1 31.1 %all-to-all-start.1 = ((bf16[16,22,1024]{2,1,0:T(8,128)(2,1)}), bf16[16,22,1024]{2,1,0:T(8,128)(2,1)S(1)}, u32[]{:S(2)}, u32[]{:S(2)}) async-start(bf16[16,22,1024]{2,1,0:T(8,128)(2,1)} %reshape.168), calls=%async_computation.2 | async-start | bytes 1572864 | tf_op jit(solution)/shard_map/all_to_all | solution.py:99
  445.2 22.7 %copy-start.21 = (f32[1024]{0:T(1024)S(1)}, f32[1024]{0:T(1024)}, u32[]{:S(2)}) copy-start(f32[1024]{0:T(1024)} %param.19) | copy-start | bytes 12292
  (9 other events, 72.0 us)
Sparse Core Ops, SparseCore 0:
  11.9 87.6 reduce-scatter.6
  340.6 93.2 reduce-scatter.4
